TPU v7x, 256 devices: a whole 4x4x8 slice. The times are simulated.
256 devices in a mesh: tiles: 64 (over z, x, core), views: 4 (over y).
Axes of the slice: x: 4, y: 4, z: 8, core: 2. Of those that a mesh axis runs over, the one named last changes fastest.
Arguments:
- gaussians: float32 [59, 131072], P(None, 'tiles')
- moment_one: float32 [59, 131072], P(None, 'tiles'), may hold values from -3 to 3
- moment_two: float32 [59, 131072], P(None, 'tiles'), may hold values from 0.01 to 1
- learn_rates: float32 [59], replicated, may hold values from 0.002 to 0.05
- cameras: float32 [16, 12], replicated, as said below
- camera_ids: int32 [4], P('views'), may hold values from 0 to 15
- list_owner: int32 [4, 64, 1024, 1], P('views', 'tiles'), may hold values from 0 to 63; in each aligned block of 1024 rows (0 to 1023, 1024 to 2047, ..., all dimensions but the last counted through in order) at most 32 rows name the same one
- list_index: int32 [4, 64, 1024], P('views', 'tiles'), may hold values from 0 to 2047
- list_length: int32 [4, 64], P('views', 'tiles'), may hold values from 1 to 1024, 32768 in all within a row
- targets: bfloat16 [4, 64, 3, 1024], P('views', 'tiles'), may hold values from 0 to 1
- background: float32 [3], replicated, may hold values from 0.1 to 0.9
Outputs:
- rendered: bfloat16 [4, 64, 3, 1024], P('views', 'tiles')
- new_gaussians: float32 [59, 131072], P(None, 'tiles')
- new_moment_one: float32 [59, 131072], P(None, 'tiles')
- new_moment_two: float32 [59, 131072], P(None, 'tiles')
Inputs may be any that keep to these rules, and one draw needn't show every extreme that they name: `list_owner`: in the list of one device (one camera slot, one tile) no owner is named by more than 32 entries, and some device's list reaches this bound. `cameras`: rotations are proper, and every Gaussian lies in front of every camera.
All inputs are finite; a program needn't handle non-finite values. No bound on the sum of `list_length` on one device may be relied on, other than what follows from the above.
Results may differ from a plain program's by a relative error of at most 0.001.
Values sent between devices are 32-bit elements; how exact they have to be, the bound alone decides.
No kernel may reach another device: no remote copies, remote signals or barrier semaphores. Data moves between devices by JAX's collectives and lax.ppermute only.
A program may use at most 192 MiB of HBM per device.

v0:
```python
from functools import partial
import jax
import jax.numpy as jnp
from jax import lax
from jax.sharding import PartitionSpec as P

TILE_SIDE = 32
PIXELS = 1024
TILE_ROWS = 8
LIST = 1024
BLOCK = 128
focal_length = 400.0
precise = lax.Precision.HIGHEST
decay_one = 0.9
decay_two = 0.999
adam_epsilon = 1e-08


def sh_basis(direction):
    dir_x, dir_y, dir_z = (direction[0], direction[1], direction[2])
    sq_x, sq_y, sq_z = (dir_x * dir_x, dir_y * dir_y, dir_z * dir_z)
    terms = [
        0.28209479177387814 * jnp.ones_like(dir_x),
        -0.4886025119029199 * dir_y,
        0.4886025119029199 * dir_z,
        -0.4886025119029199 * dir_x,
        1.0925484305920792 * dir_x * dir_y,
        -1.0925484305920792 * dir_y * dir_z,
        0.31539156525252005 * (2.0 * sq_z - sq_x - sq_y),
        -1.0925484305920792 * dir_x * dir_z,
        0.5462742152960396 * (sq_x - sq_y),
        -0.5900435899266435 * dir_y * (3.0 * sq_x - sq_y),
        2.890611442640554 * dir_x * dir_y * dir_z,
        -0.4570457994644658 * dir_y * (4.0 * sq_z - sq_x - sq_y),
        0.3731763325901154 * dir_z * (2.0 * sq_z - 3.0 * sq_x - 3.0 * sq_y),
        -0.4570457994644658 * dir_x * (4.0 * sq_z - sq_x - sq_y),
        1.445305721320277 * dir_z * (sq_x - sq_y),
        -0.5900435899266435 * dir_x * (sq_x - 3.0 * sq_y),
    ]
    return jnp.stack(terms)


def quat_rotation(quat):
    length = jnp.sqrt(jnp.sum(quat * quat, axis=0))
    quat_w, quat_x, quat_y, quat_z = (
        quat[0] / length,
        quat[1] / length,
        quat[2] / length,
        quat[3] / length,
    )
    rows = [
        [
            1.0 - 2.0 * (quat_y * quat_y + quat_z * quat_z),
            2.0 * (quat_x * quat_y - quat_w * quat_z),
            2.0 * (quat_x * quat_z + quat_w * quat_y),
        ],
        [
            2.0 * (quat_x * quat_y + quat_w * quat_z),
            1.0 - 2.0 * (quat_x * quat_x + quat_z * quat_z),
            2.0 * (quat_y * quat_z - quat_w * quat_x),
        ],
        [
            2.0 * (quat_x * quat_z - quat_w * quat_y),
            2.0 * (quat_y * quat_z + quat_w * quat_x),
            1.0 - 2.0 * (quat_x * quat_x + quat_y * quat_y),
        ],
    ]
    return jnp.stack([jnp.stack(entries) for entries in rows])


def project(params, camera, center_x, center_y):
    means = params[0:3]
    rotate = camera[0:9].reshape(3, 3)
    shift = camera[9:12]
    view_pos = jnp.dot(rotate, means, precision=precise) + shift[:, None]
    inv_depth = 1.0 / view_pos[2]
    image_x = focal_length * view_pos[0] * inv_depth + center_x
    image_y = focal_length * view_pos[1] * inv_depth + center_y
    scales = jnp.exp(params[3:6])
    local_axes = quat_rotation(params[6:10]) * scales[None, :, :]
    world_axes = jnp.einsum("ik,kjg->ijg", rotate, local_axes, precision=precise)
    proj_x = (
        focal_length * inv_depth * world_axes[0]
        - focal_length * view_pos[0] * inv_depth * inv_depth * world_axes[2]
    )
    proj_y = (
        focal_length * inv_depth * world_axes[1]
        - focal_length * view_pos[1] * inv_depth * inv_depth * world_axes[2]
    )
    cov_xx = jnp.sum(proj_x * proj_x, axis=0) + 0.3
    cov_xy = jnp.sum(proj_x * proj_y, axis=0)
    cov_yy = jnp.sum(proj_y * proj_y, axis=0) + 0.3
    determ = cov_xx * cov_yy - cov_xy * cov_xy
    opacity = 0.99 * jax.nn.sigmoid(params[10])
    center = -jnp.dot(rotate.T, shift, precision=precise)
    offset = means - center[:, None]
    direction = offset / jnp.sqrt(jnp.sum(offset * offset, axis=0))
    basis = sh_basis(direction)
    coeffs = params[11:59].reshape(16, 3, -1)
    colors = 0.5 + jnp.sum(basis[:, None, :] * coeffs, axis=0)
    head = jnp.stack(
        [image_x, image_y, cov_yy / determ, -cov_xy / determ, cov_xx / determ, opacity]
    )
    return jnp.concatenate([head, colors], axis=0)


def pixel_grid(tile, tile_cols):
    offsets = jnp.arange(PIXELS)
    pixel_x = (tile % tile_cols * TILE_SIDE + offsets % TILE_SIDE).astype(jnp.float32) + 0.5
    pixel_y = (tile // tile_cols * TILE_SIDE + offsets // TILE_SIDE).astype(jnp.float32) + 0.5
    return (pixel_x, pixel_y)


def block_terms(entry, count, pixel_x, pixel_y, index):
    start = index * BLOCK
    piece = lax.dynamic_slice_in_dim(entry, start, BLOCK, 1)
    live = (start + jnp.arange(BLOCK) < count)[None, :]
    delta_x = pixel_x[:, None] - piece[0][None, :]
    delta_y = pixel_y[:, None] - piece[1][None, :]
    power = -0.5 * (
        piece[2] * delta_x * delta_x
        + 2.0 * piece[3] * delta_x * delta_y
        + piece[4] * delta_y * delta_y
    )
    falloff = jnp.exp(power)
    alpha = jnp.where(live, piece[5][None, :] * falloff, 0.0)
    log_keep = jnp.log1p(-alpha)
    return (start, piece, live, delta_x, delta_y, falloff, alpha, log_keep)


def tile_pass(entry, count, pixel_x, pixel_y, target, background):
    blocks = (count + BLOCK - 1) // BLOCK

    def forward(index, carry):
        color, log_total = carry
        start, piece, live, delta_x, delta_y, falloff, alpha, log_keep = block_terms(
            entry, count, pixel_x, pixel_y, index
        )
        weight = jnp.exp(log_total[:, None] + jnp.cumsum(log_keep, axis=1) - log_keep) * alpha
        color = color + lax.dot_general(
            piece[6:9], weight, (((1,), (1,)), ((), ())), precision=precise
        )
        return (color, log_total + jnp.sum(log_keep, axis=1))

    zeros_pix = jnp.zeros((PIXELS,), jnp.float32)
    color, log_total = lax.fori_loop(
        0, blocks, forward, (jnp.zeros((3, PIXELS), jnp.float32), zeros_pix)
    )
    image = color + jnp.exp(log_total)[None, :] * background[:, None]
    resid = image - target
    dot_total = jnp.sum(image * resid, axis=0)

    def backward(index, carry):
        grads, log_before, prefix = carry
        start, piece, live, delta_x, delta_y, falloff, alpha, log_keep = block_terms(
            entry, count, pixel_x, pixel_y, index
        )
        trans = jnp.exp(log_before[:, None] + jnp.cumsum(log_keep, axis=1) - log_keep)
        weight = trans * alpha
        along = lax.dot_general(resid, piece[6:9], (((0,), (0,)), ((), ())), precision=precise)
        running = prefix[:, None] + jnp.cumsum(weight * along, axis=1)
        d_alpha = jnp.where(
            live, trans * along - (dot_total[:, None] - running) / (1.0 - alpha), 0.0
        )
        d_power = d_alpha * alpha
        sum_x = jnp.sum(d_power * delta_x, axis=0)
        sum_y = jnp.sum(d_power * delta_y, axis=0)
        head = jnp.stack(
            [
                piece[2] * sum_x + piece[3] * sum_y,
                piece[3] * sum_x + piece[4] * sum_y,
                -0.5 * jnp.sum(d_power * delta_x * delta_x, axis=0),
                -jnp.sum(d_power * delta_x * delta_y, axis=0),
                -0.5 * jnp.sum(d_power * delta_y * delta_y, axis=0),
                jnp.sum(d_alpha * falloff, axis=0),
            ]
        )
        color_grad = jnp.dot(resid, weight, precision=precise)
        block_grad = jnp.concatenate([head, color_grad], axis=0)
        grads = lax.dynamic_update_slice_in_dim(grads, block_grad, start, 1)
        return (grads, log_before + jnp.sum(log_keep, axis=1), running[:, -1])

    start_grads = jnp.zeros((9, LIST), jnp.float32)
    grads, ignored, unused = lax.fori_loop(0, blocks, backward, (start_grads, zeros_pix, zeros_pix))
    return (image, grads)


def adam_step(values, first, second, grad, rates):
    first_new = decay_one * first + (1.0 - decay_one) * grad
    second_new = decay_two * second + (1.0 - decay_two) * grad * grad
    return (
        values - rates[:, None] * first_new / (jnp.sqrt(second_new) + adam_epsilon),
        first_new,
        second_new,
    )


def body(
    gaussians,
    moment_one,
    moment_two,
    learn_rates,
    cameras,
    camera_ids,
    list_owner,
    list_index,
    list_length,
    targets,
    background,
):
    peers = lax.axis_size("tiles")
    tiles_here = list_index.shape[1]
    entries = tiles_here * LIST
    owned = gaussians.shape[1]
    capacity = 2 * entries // peers
    tile_cols = tiles_here * peers // TILE_ROWS
    center_x = 0.5 * TILE_SIDE * tile_cols
    center_y = 0.5 * TILE_SIDE * TILE_ROWS
    camera = cameras[camera_ids[0]]
    attrs, pullback = jax.vjp(
        partial(project, camera=camera, center_x=center_x, center_y=center_y), gaussians
    )
    owner_flat = list_owner.reshape(-1)
    index_flat = list_index.reshape(-1)
    order = jnp.argsort(owner_flat, stable=True)
    sorted_owner = owner_flat[order]
    one_hot = (sorted_owner[:, None] == jnp.arange(peers)[None, :]).astype(jnp.int32)
    counts = jnp.sum(one_hot, axis=0)
    starts = jnp.cumsum(counts) - counts
    rank = jnp.arange(entries) - jnp.sum(one_hot * starts[None, :], axis=1)
    slot = sorted_owner * capacity + rank
    position = jnp.zeros((entries,), jnp.int32).at[order].set(slot)
    asked_for = (
        jnp.zeros((peers * capacity,), jnp.int32)
        .at[slot]
        .set(index_flat[order])
        .reshape(peers, capacity)
    )
    asked = lax.all_to_all(asked_for, "tiles", split_axis=0, concat_axis=0, tiled=True)
    served = jnp.take(attrs, asked, axis=1)
    returned = lax.all_to_all(served, "tiles", split_axis=1, concat_axis=1, tiled=True)
    entry_attrs = returned.reshape(9, peers * capacity)[:, position].reshape(9, tiles_here, LIST)
    first_tile = lax.axis_index("tiles") * tiles_here

    def render(item):
        local_tile, entry, count, target = item
        pixel_x, pixel_y = pixel_grid(first_tile + local_tile, tile_cols)
        return tile_pass(entry, count, pixel_x, pixel_y, target.astype(jnp.float32), background)

    images, tile_grads = lax.map(
        render,
        (jnp.arange(tiles_here), jnp.moveaxis(entry_attrs, 1, 0), list_length[0], targets[0]),
    )
    flat_grads = jnp.moveaxis(tile_grads, 0, 1).reshape(9, entries)
    global_ids = owner_flat * owned + index_flat
    dense = jnp.zeros((9, peers * owned), jnp.float32).at[:, global_ids].add(flat_grads)
    attr_grad = lax.psum_scatter(dense, "tiles", scatter_dimension=1, tiled=True)
    param_grad = pullback(attr_grad)[0]
    total = lax.psum(param_grad, "views")
    new_values, first_new, second_new = adam_step(
        gaussians, moment_one, moment_two, total, learn_rates
    )
    return (images[None].astype(jnp.bfloat16), new_values, first_new, second_new)


def solution(mesh):
    return jax.shard_map(
        body,
        mesh=mesh,
        in_specs=(
            P(None, "tiles"),
            P(None, "tiles"),
            P(None, "tiles"),
            P(),
            P(),
            P("views"),
            P("views", "tiles", None, None),
            P("views", "tiles", None),
            P("views", "tiles"),
            P("views", "tiles", None, None),
            P(),
        ),
        out_specs=(
            P("views", "tiles", None, None),
            P(None, "tiles"),
            P(None, "tiles"),
            P(None, "tiles"),
        ),
        check_vma=False,
    )
```

profile of v0, /device:TPU:2, one launch (start us, length us, event | category | flops | bytes accessed | tf_op | source)
XLA Modules:
  0.0 475.0 jit_solution(15722905798426778904)
XLA Ops:
  7.2 5.1 %sort.17 = (s32[1024]{0:T(1024)}, s32[1024]{0:T(1024)S(1)}) sort(s32[1024]{0:T(1024)} %bitcast.355, s32[1024]{0:T(1024)S(1)} %iota.30), dimensions={0}, to_apply=%region_0.0 | sort | flops 10240 | bytes 16384 | tf_op jit(solution)/shard_map/jit(argsort)/sort | solution.py:225
  12.3 5.7 %gather_fusion = s32[1024]{0:T(1024)S(1)} fusion(s32[1024]{0:T(1024)} %bitcast.356, s32[1024]{0:T(1024)S(1)} %get-tuple-element.458), kind=kCustom, calls=%fused_computation | custom fusion | bytes 12288 | tf_op jit(solution)/shard_map/gather | solution.py:226
  18.0 5.7 %gather_fusion.1 = s32[1024]{0:T(1024)S(1)} fusion(s32[1024]{0:T(1024)} %bitcast.357, s32[1024]{0:T(1024)S(1)} %get-tuple-element.458), kind=kCustom, calls=%fused_computation.1 | custom fusion | bytes 12288 | tf_op jit(solution)/shard_map/gather | solution.py:236
  24.3 4.3 scatter_custom_fusion
  29.3 12.0 %all-to-all-start = ((s32[64,1,32]{2,1,0:T(1,128)}), s32[64,1,32]{2,1,0:T(1,128)S(1)}, u32[]{:S(2)}, u32[]{:S(2)}) async-start(s32[64,1,32]{2,1,0:T(1,128)} %bitcast.7), calls=%async_computation | async-start | bytes 65536 | tf_op jit(solution)/shard_map/all_to_all | solution.py:239
  43.8 1.1 slice.164
  46.2 1.0 convolution_add_fusion.2
  47.3 1.0 broadcast_divide_fusion
  48.3 1.7 broadcast_multiply_fusion.10
  52.3 4.4 sort.18
  58.6 4.3 scatter_custom_fusion.1
  63.0 5.5 %gather_fusion.2 = f32[2048,9]{1,0:T(8,128)S(1)} fusion(f32[9,2048]{0,1:T(8,128)S(1)} %copy.61, s32[2048]{0:T(1024)S(1)} %broadcast_clamp_fusion), kind=kCustom, calls=%fused_computation.2 | custom fusion | bytes 155648 | tf_op jit(solution)/shard_map/jit(_take)/gather | solution.py:240
  69.9 10.3 %all-to-all-start.1 = ((f32[64,1,288]{2,1,0:T(1,128)}), f32[64,1,288]{2,1,0:T(1,128)S(1)}, u32[]{:S(2)}, u32[]{:S(2)}) async-start(f32[64,1,288]{2,1,0:T(1,128)} %reshape.822), calls=%async_computation.1 | async-start | bytes 196608 | tf_op jit(solution)/shard_map/all_to_all | solution.py:241
  80.3 9.3 %all-to-all-done.1 = f32[64,1,288]{2,1,0:T(1,128)S(1)} async-done(((f32[64,1,288]{2,1,0:T(1,128)}), f32[64,1,288]{2,1,0:T(1,128)S(1)}, u32[]{:S(2)}, u32[]{:S(2)}) %all-to-all-start.1) | async-done | bytes 73760 | tf_op jit(solution)/shard_map/all_to_all | solution.py:241
  91.6 2.8 gather_fusion.3
  94.6 22.7 %while.40 = (s32[]{:T(128)}, f32[3,1024]{1,0:T(4,128)S(1)}, f32[1024]{0:T(1024)S(1)}, s32[]{:T(128)}, f32[9,1024]{1,0:T(8,128)S(1)}, /*index=5*/s32[]{:T(128)}, ...) while((s32[]{:T(128)}, f32[3,1024]{1,0:T(4,128)S(1)}, ...), condition=%wide.region_15.16_spmd.clone, body=%wide.region_12.15_spmd.clone.sunk | while | flops 25580940 | bytes 2186327 | solution.py:146
  96.9 1.0 convolution_add_fusion.4
  99.6 1.0 convolution_add_fusion.4
  102.4 1.0 convolution_add_fusion.4
  105.2 1.0 convolution_add_fusion.4
  108.0 1.0 convolution_add_fusion.4
  110.7 1.0 convolution_add_fusion.4
  116.3 1.0 convolution_add_fusion.4
  117.3 1.4 multiply_reduce_fusion.10
  118.7 65.1 %while.41 = (s32[]{:T(128)}, f32[9,1024]{1,0:T(8,128)S(1)}, f32[1024]{0:T(1024)S(1)}, f32[1024]{0:T(1024)S(1)}, s32[]{:T(128)}, /*index=5*/f32[9,1024]{1,0:T(8,1...) while((s32[]{:T(128)}, f32[9,1024]{1,0:T(8,128)S(1)}, ...), condition=%wide.region_27.28_spmd.clone, body=%wide.region_17.27_spmd.clone.sunk | while | flops 55855884 | bytes 9094147 | solution.py:184
  120.5 1.8 convolution_bitcast_fusion.4
  122.3 2.0 fusion.212
  128.6 1.8 convolution_bitcast_fusion.4
  130.4 2.0 fusion.212
  136.7 1.8 convolution_bitcast_fusion.4
  138.5 2.0 fusion.212
  144.8 1.8 convolution_bitcast_fusion.4
  146.6 2.0 fusion.212
  153.0 1.8 convolution_bitcast_fusion.4
  154.7 2.0 fusion.212
  161.1 1.8 convolution_bitcast_fusion.4
  162.9 2.0 fusion.212
  169.2 1.8 convolution_bitcast_fusion.4
  171.0 2.0 fusion.212
  177.3 1.8 convolution_bitcast_fusion.4
  179.1 2.0 fusion.212
  184.1 42.6 %scatter_custom_fusion.2 = f32[9,131072]{0,1:T(8,128)} fusion(s32[1024]{0:T(1024)} %get-tuple-element.261, f32[]{:T(128)} %constant.125.clone.1, f32[1024,9]{1,0:T(8,128)S(1)} %copy.66, s32[1024]{0:T(1024)} %broadcast_clamp_fusion.1), kind=kCustom, calls=%fused_computation.125 | custom fusion | flops 9216 | bytes 4719104 | tf_op jit(solution)/shard_map/scatter-add | solution.py:256
  226.8 36.9 %copy.67 = f32[9,131072]{1,0:T(8,128)} copy(f32[9,131072]{0,1:T(8,128)} %scatter_custom_fusion.2) | data formatting | bytes 9437184 | tf_op jit(solution)/shard_map/scatter-add | solution.py:256
  263.8 147.5 %reduce-scatter.2.cloned.1.call-done = f32[9,2048]{1,0:T(8,128)} async-done(((f32[9,131072]{1,0:T(8,128)}), f32[9,2048]{1,0:T(8,128)}) %reduce-scatter.2.cloned.1.call-update) | async-done | bytes 73744 | tf_op jit(solution)/shard_map/reduce_scatter | solution.py:257
  413.2 1.0 fusion.183
  415.9 1.1 multiply_multiply_fusion.2
  418.1 47.4 %all-reduce.23.cloned.1.call-done = f32[59,2048]{1,0:T(8,128)} async-done(((f32[59,2048]{1,0:T(8,128)}), f32[59,2048]{1,0:T(8,128)}) %all-reduce.23.cloned.1.call-update) | async-done | bytes 483344 | tf_op jit(solution)/shard_map/psum | solution.py:259
  465.5 2.4 divide_subtract_fusion
  (292 shorter events, 65.8 us)
Async XLA Ops:
  7.2 34.8 %copy-start = (f32[16,12]{1,0:T(8,128)S(1)}, f32[16,12]{1,0:T(8,128)}, u32[]{:S(2)}) copy-start(f32[16,12]{1,0:T(8,128)} %param.19) | copy-start | bytes 2308
  29.3 33.6 %all-to-all-start = ((s32[64,1,32]{2,1,0:T(1,128)}), s32[64,1,32]{2,1,0:T(1,128)S(1)}, u32[]{:S(2)}, u32[]{:S(2)}) async-start(s32[64,1,32]{2,1,0:T(1,128)} %bitcast.7), calls=%async_computation | async-start | bytes 65536 | tf_op jit(solution)/shard_map/all_to_all | solution.py:239
  45.2 3.1 copy-start.6
  69.9 19.7 %all-to-all-start.1 = ((f32[64,1,288]{2,1,0:T(1,128)}), f32[64,1,288]{2,1,0:T(1,128)S(1)}, u32[]{:S(2)}, u32[]{:S(2)}) async-start(f32[64,1,288]{2,1,0:T(1,128)} %reshape.822), calls=%async_computation.1 | async-start | bytes 196608 | tf_op jit(solution)/shard_map/all_to_all | solution.py:241
  80.2 331.1 %reduce-scatter.2.cloned.1.call-start = ((), (), s32[]{:S(2)}) async-start(), calls=%async_computation.3 | async-start | bytes 8519680 | tf_op jit(solution)/shard_map/reduce_scatter | solution.py:257
  184.0 231.6 %copy-start.1 = (f32[59,2048]{1,0:T(8,128)S(1)}, f32[59,2048]{1,0:T(8,128)}, u32[]{:S(2)}) copy-start(f32[59,2048]{1,0:T(8,128)} %param.15) | copy-start | bytes 1449988
  184.1 231.6 %copy-start.7 = (f32[3]{0:T(128)S(1)}, f32[3]{0:T(128)}, u32[]{:S(2)}) copy-start(f32[3]{0:T(128)} %copy-done.6) | copy-start | bytes 40
  184.1 231.7 %copy-start.4 = (f32[1,2048]{1,0:T(1,128)S(1)}, f32[1,2048]{1,0:T(1,128)}, u32[]{:S(2)}) copy-start(f32[1,2048]{1,0:T(1,128)} %get-tuple-element.381) | copy-start | bytes 24580
  184.1 231.7 %copy-start.5 = (f32[1,2048]{1,0:T(1,128)S(1)}, f32[1,2048]{1,0:T(1,128)}, u32[]{:S(2)}) copy-start(f32[1,2048]{1,0:T(1,128)} %get-tuple-element.382) | copy-start | bytes 24580
  184.1 281.4 %copy-start.2 = (f32[59,2048]{1,0:T(8,128)S(1)}, f32[59,2048]{1,0:T(8,128)}, u32[]{:S(2)}) copy-start(f32[59,2048]{1,0:T(8,128)} %param.16) | copy-start | bytes 1449988
  184.1 281.4 %copy-start.3 = (f32[59,2048]{1,0:T(8,128)S(1)}, f32[59,2048]{1,0:T(8,128)}, u32[]{:S(2)}) copy-start(f32[59,2048]{1,0:T(8,128)} %param.17) | copy-start | bytes 1449988
  184.1 281.4 %copy-start.8 = (f32[59]{0:T(128)S(1)}, f32[59]{0:T(128)}, u32[]{:S(2)}) copy-start(f32[59]{0:T(128)} %param.18) | copy-start | bytes 712
  263.7 201.8 %all-reduce.23.cloned.1.call-start = ((), (), s32[]{:S(2)}) async-start(), calls=%async_computation.4 | async-start | bytes 1048576 | tf_op jit(solution)/shard_map/psum | solution.py:259
Sparse Core Ops, SparseCore 0:
  263.9 147.4 reduce-scatter.1
  418.3 47.2 all-reduce.22
where the time goes:
time: 485 us; the launch traced here: 475 us
  waiting for transfers between devices  204 us (42%)
  other arithmetic  116 us (24%)
  local copies, waits for them, and re-layouts  74.5 us (15%)
  matrix products  40 us (8%)
  starting transfers between devices  22.4 us (5%)
  between operations  16.3 us (3%)
    reduce_scatter x1, waiting for transfers between devices, body(): lax.psum_scatter(dense, 'tiles', scatter_dimension=1, tiled=True)  148 us
    scatter-add x3, other arithmetic, body(): jnp.zeros((9, peers * owned), jnp.float32).at[:, global_ids].add(flat_grads)  47.6 us
    psum x1, waiting for transfers between devices, body(): total = lax.psum(param_grad, 'views')  47.4 us
    scatter-add x2, local copies, waits for them, and re-layouts, body(): jnp.zeros((9, peers * owned), jnp.float32).at[:, global_ids].add(flat_grads)  36.9 us
    dot_general x8, matrix products, backward(): lax.dot_general(resid, piece[6:9], (((0,), (0,)), ((), ())), precision=pr...  15.8 us
    dot_general x8, matrix products, backward(): color_grad = jnp.dot(resid, weight, precision=precise)  14.4 us
    all_to_all x1, starting transfers between devices, body(): lax.all_to_all(asked_for, 'tiles', split_axis=0, concat_axis=0, tiled=True)  12 us
    lt x16, other arithmetic, block_terms(): live = (start + jnp.arange(BLOCK) < count)[None, :]  10.5 us
  transfers between devices with their start and end apart: 4, of which 3 were waited for; matrix products, arithmetic and copies ran while one was open for 4% of the time, Pallas kernels for 0%

commit v1 on v0

--- a/solution.py
+++ b/solution.py
@@ -256,7 +256,9 @@
     dense = jnp.zeros((9, peers * owned), jnp.float32).at[:, global_ids].add(flat_grads)
     attr_grad = lax.psum_scatter(dense, "tiles", scatter_dimension=1, tiled=True)
     param_grad = pullback(attr_grad)[0]
-    total = lax.psum(param_grad, "views")
+    total = param_grad
+    for hop in (1, 2):
+        total = total + lax.ppermute(total, "views", [(dev, dev ^ hop) for dev in range(4)])
     new_values, first_new, second_new = adam_step(
         gaussians, moment_one, moment_two, total, learn_rates
     )

time: 485 us -> 448 us (0.924)
  the two profiles are of different devices: /device:TPU:2 before, /device:TPU:24 now
where the time goes in v1:
time: 448 us; the launch traced here: 440 us
  waiting for transfers between devices  190 us (42%)
  other arithmetic  107 us (24%)
  local copies, waits for them, and re-layouts  75.9 us (17%)
  matrix products  25.2 us (6%)
  starting transfers between devices  23.3 us (5%)
  between operations  16.7 us (4%)
    reduce_scatter x1, waiting for transfers between devices, body(): lax.psum_scatter(dense, 'tiles', scatter_dimension=1, tiled=True)  157 us
    scatter-add x3, other arithmetic, body(): jnp.zeros((9, peers * owned), jnp.float32).at[:, global_ids].add(flat_grads)  46.2 us
    scatter-add x2, local copies, waits for them, and re-layouts, body(): jnp.zeros((9, peers * owned), jnp.float32).at[:, global_ids].add(flat_grads)  37.1 us
    ppermute x2, waiting for transfers between devices, body(): lax.ppermute(total, 'views', [(dev, dev ^ hop) for dev in range(4)])  22.8 us
    all_to_all x1, starting transfers between devices, body(): lax.all_to_all(asked_for, 'tiles', split_axis=0, concat_axis=0, tiled=True)  11.9 us
    all_to_all x1, waiting for transfers between devices, body(): lax.all_to_all(served, 'tiles', split_axis=1, concat_axis=1, tiled=True)  10.5 us
    all_to_all x1, starting transfers between devices, body(): lax.all_to_all(served, 'tiles', split_axis=1, concat_axis=1, tiled=True)  10.3 us
    lt x14, other arithmetic, block_terms(): live = (start + jnp.arange(BLOCK) < count)[None, :]  9.14 us
  transfers between devices with their start and end apart: 5, of which 4 were waited for; matrix products, arithmetic and copies ran while one was open for 4% of the time, Pallas kernels for 0%

profile of v1, /device:TPU:24, one launch (start us, length us, event | category | flops | bytes accessed | tf_op | source)
XLA Modules:
  0.0 439.6 jit_solution(12599499597651002821)
XLA Ops:
  7.2 5.1 %sort.17 = (s32[1024]{0:T(1024)}, s32[1024]{0:T(1024)S(1)}) sort(s32[1024]{0:T(1024)} %bitcast.355, s32[1024]{0:T(1024)S(1)} %iota.30), dimensions={0}, to_apply=%region_0.0 | sort | flops 10240 | bytes 16384 | tf_op jit(solution)/shard_map/jit(argsort)/sort | solution.py:225
  12.3 5.7 %gather_fusion = s32[1024]{0:T(1024)S(1)} fusion(s32[1024]{0:T(1024)} %bitcast.356, s32[1024]{0:T(1024)S(1)} %get-tuple-element.458), kind=kCustom, calls=%fused_computation | custom fusion | bytes 12288 | tf_op jit(solution)/shard_map/gather | solution.py:226
  18.0 5.7 %gather_fusion.1 = s32[1024]{0:T(1024)S(1)} fusion(s32[1024]{0:T(1024)} %bitcast.357, s32[1024]{0:T(1024)S(1)} %get-tuple-element.458), kind=kCustom, calls=%fused_computation.1 | custom fusion | bytes 12288 | tf_op jit(solution)/shard_map/gather | solution.py:236
  24.3 4.3 scatter_custom_fusion
  29.3 11.9 %all-to-all-start = ((s32[64,1,32]{2,1,0:T(1,128)}), s32[64,1,32]{2,1,0:T(1,128)S(1)}, u32[]{:S(2)}, u32[]{:S(2)}) async-start(s32[64,1,32]{2,1,0:T(1,128)} %bitcast.7), calls=%async_computation | async-start | bytes 65536 | tf_op jit(solution)/shard_map/all_to_all | solution.py:239
  43.7 1.1 slice.164
  46.1 1.0 convolution_add_fusion.2
  47.2 1.0 broadcast_divide_fusion
  48.2 1.1 broadcast_multiply_fusion.10
  53.7 3.8 sort.18
  58.8 4.3 scatter_custom_fusion.1
  63.2 5.5 %gather_fusion.2 = f32[2048,9]{1,0:T(8,128)S(1)} fusion(f32[9,2048]{0,1:T(8,128)S(1)} %copy.61, s32[2048]{0:T(1024)S(1)} %broadcast_clamp_fusion), kind=kCustom, calls=%fused_computation.2 | custom fusion | bytes 155648 | tf_op jit(solution)/shard_map/jit(_take)/gather | solution.py:240
  70.1 10.3 %all-to-all-start.1 = ((f32[64,1,288]{2,1,0:T(1,128)}), f32[64,1,288]{2,1,0:T(1,128)S(1)}, u32[]{:S(2)}, u32[]{:S(2)}) async-start(f32[64,1,288]{2,1,0:T(1,128)} %reshape.822), calls=%async_computation.1 | async-start | bytes 196608 | tf_op jit(solution)/shard_map/all_to_all | solution.py:241
  80.5 10.5 %all-to-all-done.1 = f32[64,1,288]{2,1,0:T(1,128)S(1)} async-done(((f32[64,1,288]{2,1,0:T(1,128)}), f32[64,1,288]{2,1,0:T(1,128)S(1)}, u32[]{:S(2)}, u32[]{:S(2)}) %all-to-all-start.1) | async-done | bytes 73760 | tf_op jit(solution)/shard_map/all_to_all | solution.py:241
  92.9 2.8 gather_fusion.3
  96.0 19.9 %while.40 = (s32[]{:T(128)}, f32[3,1024]{1,0:T(4,128)S(1)}, f32[1024]{0:T(1024)S(1)}, s32[]{:T(128)}, f32[9,1024]{1,0:T(8,128)S(1)}, /*index=5*/s32[]{:T(128)}, ...) while((s32[]{:T(128)}, f32[3,1024]{1,0:T(4,128)S(1)}, ...), condition=%wide.region_15.16_spmd.clone, body=%wide.region_12.15_spmd.clone.sunk | while | flops 25580940 | bytes 2186327 | solution.py:146
  98.2 1.0 convolution_add_fusion.4
  101.0 1.0 convolution_add_fusion.4
  103.8 1.0 convolution_add_fusion.4
  106.6 1.0 convolution_add_fusion.4
  109.3 1.0 convolution_add_fusion.4
  112.1 1.0 convolution_add_fusion.4
  114.9 1.0 convolution_add_fusion.4
  115.9 1.4 multiply_reduce_fusion.10
  117.3 46.9 %while.41 = (s32[]{:T(128)}, f32[9,1024]{1,0:T(8,128)S(1)}, f32[1024]{0:T(1024)S(1)}, f32[1024]{0:T(1024)S(1)}, s32[]{:T(128)}, /*index=5*/f32[9,1024]{1,0:T(8,1...) while((s32[]{:T(128)}, f32[9,1024]{1,0:T(8,128)S(1)}, ...), condition=%wide.region_27.28_spmd.clone, body=%wide.region_17.27_spmd.clone.sunk | while | flops 55855884 | bytes 9098243 | solution.py:184
  119.1 1.1 convolution_bitcast_fusion.4
  120.2 1.3 fusion.213
  125.8 1.1 convolution_bitcast_fusion.4
  126.9 1.3 fusion.213
  132.5 1.1 convolution_bitcast_fusion.4
  133.6 1.3 fusion.213
  139.2 1.1 convolution_bitcast_fusion.4
  140.3 1.3 fusion.213
  145.9 1.1 convolution_bitcast_fusion.4
  147.0 1.2 fusion.213
  152.6 1.1 convolution_bitcast_fusion.4
  153.6 1.3 fusion.213
  159.3 1.1 convolution_bitcast_fusion.4
  160.3 1.3 fusion.213
  164.6 42.5 %scatter_custom_fusion.2 = f32[9,131072]{0,1:T(8,128)} fusion(s32[1024]{0:T(1024)S(1)} %get-tuple-element.261, f32[]{:T(128)} %constant.125.clone.1, f32[1024,9]{1,0:T(8,128)S(1)} %copy.66, s32[1024]{0:T(1024)S(1)} %broadcast_clamp_fusion.1), kind=kCustom, calls=%fused_computation.125 | custom fusion | flops 9216 | bytes 4718596 | tf_op jit(solution)/shard_map/scatter-add | solution.py:256
  207.1 37.1 %copy.67 = f32[9,131072]{1,0:T(8,128)} copy(f32[9,131072]{0,1:T(8,128)} %scatter_custom_fusion.2) | data formatting | bytes 9437184 | tf_op jit(solution)/shard_map/scatter-add | solution.py:256
  244.3 156.7 %reduce-scatter.2.cloned.1.call-done = f32[9,2048]{1,0:T(8,128)} async-done(((f32[9,131072]{1,0:T(8,128)}), f32[9,2048]{1,0:T(8,128)}) %reduce-scatter.2.cloned.1.call-update) | async-done | bytes 73744 | tf_op jit(solution)/shard_map/reduce_scatter | solution.py:257
  402.8 1.0 fusion.184
  405.7 1.1 multiply_multiply_fusion.2
  407.1 1.0 collective-permute-start
  408.1 12.2 %collective-permute-done = f32[59,2048]{1,0:T(8,128)S(1)} collective-permute-done((f32[59,2048]{1,0:T(8,128)S(1)}, f32[59,2048]{1,0:T(8,128)S(1)}, u32[]{:S(2)}, u32[]{:S(2)}) %collective-permute-start) | collective-permute-done | bytes 483360 | tf_op jit(solution)/shard_map/ppermute | solution.py:261
  420.4 10.7 %collective-permute-done.1 = f32[59,2048]{1,0:T(8,128)S(1)} collective-permute-done((f32[59,2048]{1,0:T(8,128)S(1)}, f32[59,2048]{1,0:T(8,128)S(1)}, u32[]{:S(2)}, u32[]{:S(2)}) %collective-permute-start.1) | collective-permute-done | bytes 483360 | tf_op jit(solution)/shard_map/ppermute | solution.py:261
  431.1 1.4 divide_subtract_fusion
  (325 shorter events, 59.6 us)
Async XLA Ops:
  7.2 34.7 %copy-start = (f32[16,12]{1,0:T(8,128)S(1)}, f32[16,12]{1,0:T(8,128)}, u32[]{:S(2)}) copy-start(f32[16,12]{1,0:T(8,128)} %param.19) | copy-start | bytes 2308
  29.3 33.8 %all-to-all-start = ((s32[64,1,32]{2,1,0:T(1,128)}), s32[64,1,32]{2,1,0:T(1,128)S(1)}, u32[]{:S(2)}, u32[]{:S(2)}) async-start(s32[64,1,32]{2,1,0:T(1,128)} %bitcast.7), calls=%async_computation | async-start | bytes 65536 | tf_op jit(solution)/shard_map/all_to_all | solution.py:239
  46.1 5.1 %copy-start.4 = (f32[2048]{0:T(1024)}, f32[2048]{0:T(1024)S(1)}, u32[]{:S(2)}) copy-start(f32[2048]{0:T(1024)S(1)} %sqrt.40) | copy-start | bytes 24580
  47.1 4.0 copy-start.10
  47.2 6.3 %copy-start.26 = (f32[1,2048]{1,0:T(1,128)}, f32[1,2048]{1,0:T(1,128)S(1)}, u32[]{:S(2)}) copy-start(f32[1,2048]{1,0:T(1,128)S(1)} %get-tuple-element.454) | copy-start | bytes 24580
  47.2 6.3 %copy-start.28 = (f32[1,2048]{1,0:T(1,128)}, f32[1,2048]{1,0:T(1,128)S(1)}, u32[]{:S(2)}) copy-start(f32[1,2048]{1,0:T(1,128)S(1)} %get-tuple-element.412) | copy-start | bytes 24580
  49.3 1.9 copy-start.6
  49.3 1.9 copy-start.8
  49.4 0.6 copy-start.22
  50.9 0.6 copy-start.18
  50.9 0.6 copy-start.20
  52.0 65.3 %copy-start.12 = (f32[1,3,2048]{2,0,1:T(1,128)}, f32[1,3,2048]{2,0,1:T(1,128)S(1)}, u32[]{:S(2)}) copy-start(f32[1,3,2048]{2,0,1:T(1,128)S(1)} %get-tuple-element.406) | copy-start | bytes 73732
  52.0 65.3 %copy-start.14 = (f32[1,3,2048]{2,0,1:T(1,128)}, f32[1,3,2048]{2,0,1:T(1,128)S(1)}, u32[]{:S(2)}) copy-start(f32[1,3,2048]{2,0,1:T(1,128)S(1)} %get-tuple-element.407) | copy-start | bytes 73732
  52.0 65.3 %copy-start.16 = (f32[1,3,2048]{2,0,1:T(1,128)}, f32[1,3,2048]{2,0,1:T(1,128)S(1)}, u32[]{:S(2)}) copy-start(f32[1,3,2048]{2,0,1:T(1,128)S(1)} %get-tuple-element.408) | copy-start | bytes 73732
  52.7 0.6 copy-start.34
  52.7 0.8 copy-start.30
  52.7 0.8 copy-start.32
  70.1 20.8 %all-to-all-start.1 = ((f32[64,1,288]{2,1,0:T(1,128)}), f32[64,1,288]{2,1,0:T(1,128)S(1)}, u32[]{:S(2)}, u32[]{:S(2)}) async-start(f32[64,1,288]{2,1,0:T(1,128)} %reshape.822), calls=%async_computation.1 | async-start | bytes 196608 | tf_op jit(solution)/shard_map/all_to_all | solution.py:241
  80.4 320.5 %reduce-scatter.2.cloned.1.call-start = ((), (), s32[]{:S(2)}) async-start(), calls=%async_computation.3 | async-start | bytes 8519680 | tf_op jit(solution)/shard_map/reduce_scatter | solution.py:257
  164.4 237.9 %copy-start.23 = (f32[1,2048]{1,0:T(1,128)S(1)}, f32[1,2048]{1,0:T(1,128)}, u32[]{:S(2)}) copy-start(f32[1,2048]{1,0:T(1,128)} %copy-done.22) | copy-start | bytes 24580
  164.4 239.4 %copy-start.31 = (f32[2048]{0:T(1024)S(1)}, f32[2048]{0:T(1024)}, u32[]{:S(2)}) copy-start(f32[2048]{0:T(1024)} %copy-done.30) | copy-start | bytes 24580
  164.4 239.4 %copy-start.33 = (f32[2048]{0:T(1024)S(1)}, f32[2048]{0:T(1024)}, u32[]{:S(2)}) copy-start(f32[2048]{0:T(1024)} %copy-done.32) | copy-start | bytes 24580
  164.4 239.4 %copy-start.35 = (f32[2048]{0:T(1024)S(1)}, f32[2048]{0:T(1024)}, u32[]{:S(2)}) copy-start(f32[2048]{0:T(1024)} %copy-done.34) | copy-start | bytes 24580
  164.4 239.4 %copy-start.27 = (f32[1,2048]{1,0:T(1,128)S(1)}, f32[1,2048]{1,0:T(1,128)}, u32[]{:S(2)}) copy-start(f32[1,2048]{1,0:T(1,128)} %copy-done.26) | copy-start | bytes 24580
  164.5 239.4 %copy-start.29 = (f32[1,2048]{1,0:T(1,128)S(1)}, f32[1,2048]{1,0:T(1,128)}, u32[]{:S(2)}) copy-start(f32[1,2048]{1,0:T(1,128)} %copy-done.28) | copy-start | bytes 24580
  164.5 240.1 %copy-start.5 = (f32[2048]{0:T(1024)S(1)}, f32[2048]{0:T(1024)}, u32[]{:S(2)}) copy-start(f32[2048]{0:T(1024)} %copy-done.4) | copy-start | bytes 24580
  164.5 240.1 %copy-start.7 = (f32[1,2048]{1,0:T(1,128)S(1)}, f32[1,2048]{1,0:T(1,128)}, u32[]{:S(2)}) copy-start(f32[1,2048]{1,0:T(1,128)} %copy-done.6) | copy-start | bytes 24580
  164.5 240.1 %copy-start.9 = (f32[1,2048]{1,0:T(1,128)S(1)}, f32[1,2048]{1,0:T(1,128)}, u32[]{:S(2)}) copy-start(f32[1,2048]{1,0:T(1,128)} %copy-done.8) | copy-start | bytes 24580
  164.5 240.1 %copy-start.19 = (f32[1,2048]{1,0:T(1,128)S(1)}, f32[1,2048]{1,0:T(1,128)}, u32[]{:S(2)}) copy-start(f32[1,2048]{1,0:T(1,128)} %copy-done.18) | copy-start | bytes 24580
  164.5 240.1 %copy-start.21 = (f32[1,2048]{1,0:T(1,128)S(1)}, f32[1,2048]{1,0:T(1,128)}, u32[]{:S(2)}) copy-start(f32[1,2048]{1,0:T(1,128)} %copy-done.20) | copy-start | bytes 24580
  164.5 240.5 %copy-start.13 = (f32[1,3,2048]{2,0,1:T(1,128)S(1)}, f32[1,3,2048]{2,0,1:T(1,128)}, u32[]{:S(2)}) copy-start(f32[1,3,2048]{2,0,1:T(1,128)} %copy-done.12) | copy-start | bytes 73732
  164.5 240.5 %copy-start.15 = (f32[1,3,2048]{2,0,1:T(1,128)S(1)}, f32[1,3,2048]{2,0,1:T(1,128)}, u32[]{:S(2)}) copy-start(f32[1,3,2048]{2,0,1:T(1,128)} %copy-done.14) | copy-start | bytes 73732
  164.5 240.5 %copy-start.17 = (f32[1,3,2048]{2,0,1:T(1,128)S(1)}, f32[1,3,2048]{2,0,1:T(1,128)}, u32[]{:S(2)}) copy-start(f32[1,3,2048]{2,0,1:T(1,128)} %copy-done.16) | copy-start | bytes 73732
  164.5 240.5 %copy-start.24 = (f32[3,2048]{1,0:T(4,128)S(1)}, f32[3,2048]{1,0:T(4,128)}, u32[]{:S(2)}) copy-start(f32[3,2048]{1,0:T(4,128)} %get-tuple-element.338) | copy-start | bytes 73732
  164.6 240.5 %copy-start.25 = (f32[3,2048]{1,0:T(4,128)S(1)}, f32[3,2048]{1,0:T(4,128)}, u32[]{:S(2)}) copy-start(f32[3,2048]{1,0:T(4,128)} %get-tuple-element.339) | copy-start | bytes 73732
  164.6 240.9 %copy-start.1 = (f32[59,2048]{1,0:T(8,128)S(1)}, f32[59,2048]{1,0:T(8,128)}, u32[]{:S(2)}) copy-start(f32[59,2048]{1,0:T(8,128)} %param.15) | copy-start | bytes 1449988
  164.6 241.1 %copy-start.11 = (f32[3,2048]{1,0:T(4,128)S(1)}, f32[3,2048]{1,0:T(4,128)}, u32[]{:S(2)}) copy-start(f32[3,2048]{1,0:T(4,128)} %copy-done.10) | copy-start | bytes 73732
  164.6 266.5 %copy-start.2 = (f32[59,2048]{1,0:T(8,128)S(1)}, f32[59,2048]{1,0:T(8,128)}, u32[]{:S(2)}) copy-start(f32[59,2048]{1,0:T(8,128)} %param.16) | copy-start | bytes 1449988
  164.6 266.5 %copy-start.3 = (f32[59,2048]{1,0:T(8,128)S(1)}, f32[59,2048]{1,0:T(8,128)}, u32[]{:S(2)}) copy-start(f32[59,2048]{1,0:T(8,128)} %param.17) | copy-start | bytes 1449988
  164.6 266.5 %copy-start.36 = (f32[59]{0:T(128)S(1)}, f32[59]{0:T(128)}, u32[]{:S(2)}) copy-start(f32[59]{0:T(128)} %param.18) | copy-start | bytes 712
  407.1 13.1 %collective-permute-start = (f32[59,2048]{1,0:T(8,128)S(1)}, f32[59,2048]{1,0:T(8,128)S(1)}, u32[]{:S(2)}, u32[]{:S(2)}) collective-permute-start(f32[59,2048]{1,0:T(8,128)S(1)} %pad_add_fusion), channel_id=1, source_target_pairs={{0,1},{1,0},{2,3},{3,2},{4,5},{5,4},{6,7},{7,6},{8,9},{9,8},{10,11... | collective-permute-start | bytes 1449992 | tf_op jit(solution)/shard_map/ppermute | solution.py:261
  420.3 10.8 %collective-permute-start.1 = (f32[59,2048]{1,0:T(8,128)S(1)}, f32[59,2048]{1,0:T(8,128)S(1)}, u32[]{:S(2)}, u32[]{:S(2)}) collective-permute-start(f32[59,2048]{1,0:T(8,128)S(1)} %fusion.180), channel_id=1, source_target_pairs={{0,2},{1,3},{2,0},{3,1},{4,6},{5,7},{6,4},{7,5},{8,10},{9,11},{10,... | collective-permute-start | bytes 1449992 | tf_op jit(solution)/shard_map/ppermute | solution.py:261
Sparse Core Ops, SparseCore 0:
  244.4 156.5 reduce-scatter.1
